TPU v7x, 256 devices: a whole 4x4x8 slice. The times are simulated.
256 devices in a mesh: seq: 64 (over z, y, x_lo), head: 4 (over x_hi, core).
Axes of the slice: x: 4 (x_hi: 2, x_lo: 2; x = x_hi * 2 + x_lo), y: 4, z: 8, core: 2. Of those that a mesh axis runs over, the one named last changes fastest.
Arguments:
- features: bfloat16 [8192, 960], P('seq', 'head'), may hold values from -36 to 36
- conv_weight: bfloat16 [960, 120, 128], P('head'), may hold values from -0.046875 to 0.046875
- ln_gain: float32 [960], replicated, may hold values from 0.5 to 1.5
- ln_bias: float32 [960], replicated, may hold values from -4 to 4
- query_weight: bfloat16 [8, 115200], P('head'), may hold values from -0.875 to 0.875
- key_weight: bfloat16 [8, 115200], P('head'), may hold values from -0.875 to 0.875
- value_weight: bfloat16 [8, 115200], P('head'), may hold values from -0.1875 to 0.1875
- out_weight: bfloat16 [960, 960], P('head'), may hold values from -0.1875 to 0.1875
- proj_weight: bfloat16 [960, 1024], P(None, 'head'), may hold values from -0.10085894 to 0.10085894
- targets: bfloat16 [8192, 1024], P('seq', 'head'), may hold values from -3.125 to 3.125
- mask_positions: int32 [1024], P('seq'), may hold values from 0 to 8191, as said below
- distractors: int32 [1024, 100], P('seq'), may hold values from 0 to 8191, as said below
- loss_weight: float32 [1024], P('seq'), may hold values from 0.2 to 2
Outputs:
- encoded: bfloat16 [8192, 960], P('seq', 'head')
- proj_grad: float32 [960, 1024], P(None, 'head')
- target_grad: float32 [8192, 1024], P('seq', 'head')
Inputs may be any that keep to these rules, and one draw needn't show every extreme that they name: `mask_positions`: the entries of aligned block d of 16 are distinct frames of d * 128 to (d + 1) * 128 - 1. `distractors`: call value // 128 the block of an entry. In every aligned block of 16 rows exactly 50 entries name one block, the same block for all row blocks and drawn from the seed; the remaining 16 * 100 - 50 entries of the row block are spread over the other blocks as evenly as possible.
All inputs are finite; a program needn't handle non-finite values.
Results may differ from a plain program's by a relative error of at most 0.007.
Values may be sent and summed in bfloat16 or wider, within the bound.
No kernel may reach another device: no remote copies, remote signals or barrier semaphores. Data moves between devices by JAX's collectives and lax.ppermute only.
A program may use at most 128 MiB of HBM per device.

v0:
```python
import math
import jax
import jax.numpy as jnp
from jax import lax
from jax.sharding import PartitionSpec as P

TAPS = 128
NORM_EPS = 1e-05
EPSILON = 1e-06
SOFTMAX_WARMTH = 0.1


def with_halo(shard, sides, width):
    for axis, dim in sides:
        size, length = (lax.axis_size(axis), shard.shape[dim])
        up = [(i, (i + 1) % size) for i in range(size - 1)]
        down = [(j, i) for i, j in up]
        last = lax.slice_in_dim(shard, length - width, length, axis=dim)
        first = lax.slice_in_dim(shard, 0, width, axis=dim)
        before = lax.ppermute(last, axis, up)
        after = lax.ppermute(first, axis, down)
        shard = jnp.concatenate([before, shard, after], axis=dim)
    return shard


def layer_norm(hidden, gain_terms, bias_terms):
    wide = hidden.astype(jnp.float32)
    center = jnp.mean(wide, axis=-1, keepdims=True)
    spread = jnp.mean((wide - center) ** 2, axis=-1, keepdims=True)
    return ((wide - center) * lax.rsqrt(spread + NORM_EPS) * gain_terms + bias_terms).astype(
        jnp.bfloat16
    )


def head_project(normed, flat_weight, head_count, head_dim):
    full_width = normed.shape[1]
    head_weight = flat_weight.reshape(head_count, full_width, head_dim)
    result = jnp.einsum("tw,hwd->thd", normed, head_weight, preferred_element_type=jnp.float32)
    return result.astype(jnp.bfloat16)


def contrast_terms(products, target_sq, context_sq, weight_matrix):
    inv_context = lax.rsqrt(context_sq + EPSILON)
    inv_target = lax.rsqrt(target_sq + EPSILON)
    cosine_scores = products * inv_context[:, None] * inv_target
    exponentiated = jnp.exp(cosine_scores / SOFTMAX_WARMTH)
    softmax_shares = exponentiated / jnp.sum(exponentiated, axis=1, keepdims=True)
    leading_term = (lax.broadcasted_iota(jnp.int32, softmax_shares.shape, 1) == 0).astype(
        jnp.float32
    )
    logit_slope = weight_matrix[:, None] * (softmax_shares - leading_term) / SOFTMAX_WARMTH
    along = logit_slope * inv_context[:, None] * inv_target
    shrink = logit_slope * cosine_scores * inv_target * inv_target
    spread = jnp.sum(logit_slope * cosine_scores, axis=1) * inv_context * inv_context
    return (along, shrink, spread)


def attend_block(running, key_block, value_block, query_heads, head_count, score_scale):
    numer, denom, highest = running
    row_count = key_block.shape[0]
    key_heads = key_block.reshape(row_count, head_count, -1)
    value_heads = value_block.reshape(row_count, head_count, -1)
    scores = (
        jnp.einsum("qhd,khd->hqk", query_heads, key_heads, preferred_element_type=jnp.float32)
        * score_scale
    )
    new_high = jnp.maximum(highest, jnp.max(scores, axis=2))
    factor = jnp.exp(highest - new_high)
    weights = jnp.exp(scores - new_high[:, :, None])
    denom = denom * factor + jnp.sum(weights, axis=2)
    numer = numer * factor[:, :, None] + jnp.einsum(
        "hqk,khd->hqd",
        weights.astype(jnp.bfloat16),
        value_heads,
        preferred_element_type=jnp.float32,
    )
    return (numer, denom, new_high)


def take_rows(asked, targets):
    return targets[jnp.maximum(asked, 0)]


def place_rows(asked_flat, rows_flat, frame_count):
    segment_ids = jnp.where(asked_flat >= 0, asked_flat, frame_count)
    return jax.ops.segment_sum(rows_flat, segment_ids, num_segments=frame_count + 1)[:frame_count]


def per_device(
    features,
    conv_weight,
    ln_gain,
    ln_bias,
    query_weight,
    key_weight,
    value_weight,
    out_weight,
    proj_weight,
    targets,
    mask_positions,
    distractors,
    loss_weight,
):
    frame_count, local_width = features.shape
    head_dim = conv_weight.shape[1]
    head_count = local_width // head_dim
    extended = with_halo(features, (("seq", 0),), TAPS // 2)
    position = lax.conv_general_dilated(
        extended[None],
        conv_weight,
        (1,),
        "VALID",
        dimension_numbers=("NWC", "OIW", "NWC"),
        feature_group_count=head_count,
        preferred_element_type=jnp.float32,
    )[0, :frame_count]
    hidden = (features.astype(jnp.float32) + jax.nn.gelu(position, approximate=False)).astype(
        jnp.bfloat16
    )
    normed = layer_norm(lax.all_gather(hidden, "head", axis=1, tiled=True), ln_gain, ln_bias)
    query_heads = head_project(normed, query_weight, head_count, head_dim)
    key_here = head_project(normed, key_weight, head_count, head_dim).reshape(
        frame_count, local_width
    )
    value_here = head_project(normed, value_weight, head_count, head_dim).reshape(
        frame_count, local_width
    )
    score_scale = 1.0 / math.sqrt(head_dim)
    initial = (
        jnp.zeros((head_count, frame_count, head_dim), jnp.float32),
        jnp.zeros((head_count, frame_count), jnp.float32),
        jnp.full((head_count, frame_count), -1e30, jnp.float32),
    )
    running = initial
    key_piece = lax.all_gather(key_here, "seq", axis=0, tiled=True)
    value_piece = lax.all_gather(value_here, "seq", axis=0, tiled=True)
    row_count = key_piece.shape[0]

    def advance(partial_value, blocks):
        return (
            attend_block(partial_value, blocks[0], blocks[1], query_heads, head_count, score_scale),
            None,
        )

    running, _ = lax.scan(
        advance,
        running,
        (
            key_piece.reshape(row_count // 512, 512, -1),
            value_piece.reshape(row_count // 512, 512, -1),
        ),
    )
    numer, denom, _ = running
    attended = (
        (numer / denom[:, :, None])
        .astype(jnp.bfloat16)
        .transpose(1, 0, 2)
        .reshape(frame_count, local_width)
    )
    branch = lax.psum_scatter(
        jnp.dot(attended, out_weight, preferred_element_type=jnp.float32).astype(jnp.bfloat16),
        "head",
        scatter_dimension=1,
        tiled=True,
    ).astype(jnp.float32)
    encoded = (hidden.astype(jnp.float32) + branch).astype(jnp.bfloat16)
    seq_index = lax.axis_index("seq")
    seq_count = lax.axis_size("seq")
    local_mask = mask_positions - seq_index * frame_count
    masked_full = lax.all_gather(encoded[local_mask], "head", axis=1, tiled=True)
    context = jnp.dot(masked_full, proj_weight, preferred_element_type=jnp.float32)
    masked_count, distract_count = distractors.shape
    request_count = masked_count * distract_count
    capacity = 2 * request_count // seq_count
    target_width = targets.shape[1]
    flat_dist = distractors.reshape(-1)
    owners = flat_dist // frame_count
    row_ids = flat_dist % frame_count
    owner_hits = (owners[:, None] == jnp.arange(seq_count, dtype=jnp.int32)[None, :]).astype(
        jnp.int32
    )
    earlier = jnp.cumsum(owner_hits, axis=0) - owner_hits
    slot_ids = jnp.sum(earlier * owner_hits, axis=1)
    buckets = owners * capacity + slot_ids
    requests = (
        jnp.full((seq_count * capacity,), -1, jnp.int32)
        .at[buckets]
        .set(row_ids)
        .reshape(seq_count, capacity)
    )
    positive = targets[local_mask]
    asked = lax.all_to_all(requests, "seq", split_axis=0, concat_axis=0, tiled=True)
    found = take_rows(asked, targets)
    returned = lax.all_to_all(found, "seq", split_axis=0, concat_axis=0, tiled=True)
    fetched = returned.reshape(seq_count * capacity, target_width)[buckets].reshape(
        masked_count, distract_count, target_width
    )
    cands = jnp.concatenate([positive[:, None, :], fetched], axis=1).astype(jnp.float32)
    products_here = jnp.einsum("me,mke->mk", context, cands, precision=lax.Precision.HIGHEST)
    target_sq_here = jnp.sum(cands * cands, axis=2)
    context_sq_here = jnp.sum(context * context, axis=1)
    products, target_sq, context_sq = lax.psum(
        (products_here, target_sq_here, context_sq_here), "head"
    )
    along, shrink, spread = contrast_terms(products, target_sq, context_sq, loss_weight)
    cand_grads = along[:, :, None] * context[:, None, :] - shrink[:, :, None] * cands
    context_grad = (
        jnp.einsum("mk,mke->me", along, cands, precision=lax.Precision.HIGHEST)
        - spread[:, None] * context
    )
    target_grad = (
        jnp.zeros((frame_count, target_width), jnp.float32).at[local_mask].add(cand_grads[:, 0])
    )
    outgoing = (
        jnp.zeros((seq_count * capacity, target_width), jnp.float32)
        .at[buckets]
        .set(cand_grads[:, 1:].reshape(request_count, target_width))
    )
    incoming = (
        lax.all_to_all(
            outgoing.reshape(seq_count, capacity, target_width).astype(jnp.bfloat16),
            "seq",
            split_axis=0,
            concat_axis=0,
            tiled=True,
        )
        .astype(jnp.float32)
        .reshape(seq_count * capacity, target_width)
    )
    target_grad = target_grad + place_rows(asked.reshape(-1), incoming, frame_count)
    proj_term = jnp.einsum(
        "mw,me->we", masked_full.astype(jnp.float32), context_grad, precision=lax.Precision.HIGHEST
    )
    proj_grad = lax.psum(proj_term, "seq")
    return (encoded, proj_grad, target_grad)


def solution(mesh):
    return jax.shard_map(
        per_device,
        mesh=mesh,
        in_specs=(
            P("seq", "head"),
            P("head", None, None),
            P(),
            P(),
            P("head", None),
            P("head", None),
            P("head", None),
            P("head", None),
            P(None, "head"),
            P("seq", "head"),
            P("seq"),
            P("seq", None),
            P("seq"),
        ),
        out_specs=(P("seq", "head"), P(None, "head"), P("seq", "head")),
        check_vma=False,
    )
```

profile of v0, /device:TPU:8, one launch (start us, length us, event | category | flops | bytes accessed | tf_op | source)
XLA Modules:
  0.0 1307.5 jit_solution(7271690625776360250)
XLA Ops:
  8.2 3.4 collective-permute-start
  15.0 10.7 copy.41
  27.6 17.3 %fusion.67 = f32[1,129,2,120]{3,0,2,1:T(1,128)S(1)} fusion(bf16[1,256,2,120]{3,0,2,1:T(2,128)(2,1)S(1)} %copy.40, bf16[2,120,120,128]{2,1,0,3:T(8,128)(2,1)} %copy.41), kind=kOutput, calls=%fused_computation.135 | convolution fusion | flops 951091200 | bytes 7619520 | tf_op jit(solution)/shard_map/conv_general_dilated | solution.py:108
  45.3 7.2 all_gather.12
  57.4 18.1 %reduce-window.6 = s32[64,13,128]{2,1,0:T(8,128)S(1)} reduce-window(s32[64,13,128]{2,1,0:T(8,128)S(1)} %reshape.259, s32[]{:T(128)} %constant.57.clone.1), window={size=1x1x128 pad=0_0x0_0x127_0}, to_apply=%region_7.8 | reduce-window | flops 13524992 | bytes 851972 | tf_op jit(solution)/shard_map/reduce-window
  76.7 8.8 scatter_custom_fusion
  86.3 12.8 all-to-all-start
  100.6 7.8 all-to-all-done
  110.0 9.9 gather_fusion.2
  121.4 6.3 all-to-all-start.1
  128.5 194.0 %all-gather.7.cloned.1.call-done = bf16[8192,240]{0,1:T(8,128)(2,1)} async-done(((bf16[128,240]{0,1:T(8,128)(2,1)}), bf16[8192,240]{0,1:T(8,128)(2,1)}) %all-gather.7.cloned.1.call-update) | async-done | bytes 3932176 | tf_op jit(solution)/shard_map/all_gather | solution.py:136
  322.5 4.4 copy.77
  326.9 243.4 %all-gather.5.cloned.1.call-done = bf16[8192,240]{0,1:T(8,128)(2,1)} async-done(((bf16[128,240]{0,1:T(8,128)(2,1)}), bf16[8192,240]{0,1:T(8,128)(2,1)}) %all-gather.5.cloned.1.call-update) | async-done | bytes 3932176 | tf_op jit(solution)/shard_map/all_gather | solution.py:135
  570.3 4.4 copy.78
  574.8 29.4 %while.15 = (s32[]{:T(128)}, f32[2,128,120]{1,2,0:T(8,128)S(1)}, f32[2,128]{1,0:T(2,128)S(1)}, f32[2,128]{1,0:T(2,128)S(1)}, bf16[16,512,240]{1,2,0:T(8,128)(2,1...) while((s32[]{:T(128)}, f32[2,128,120]{1,2,0:T(8,128)S(1)}, ...), condition=%wide.region_5.6_spmd.clone, body=%wide.region_2.5_spmd.clone.sunk | while | flops 63794432 | bytes 3371117 | solution.py:145
  608.5 5.6 gather_fusion.3
  614.7 20.9 %reduce-scatter.2.cloned.1.call-done = bf16[128,240]{0,1:T(8,128)(2,1)} async-done(((bf16[128,960]{0,1:T(8,128)(2,1)}), bf16[128,240]{0,1:T(8,128)(2,1)}) %reduce-scatter.2.cloned.1.call-update) | async-done | bytes 61456 | tf_op jit(solution)/shard_map/reduce_scatter | solution.py:160
  637.1 6.7 all-gather.1
  645.1 13.6 %all-reduce.1 = (f32[16,101]{1,0:T(8,128)S(1)}, f32[16]{0:T(128)S(1)}, f32[16,101]{1,0:T(8,128)S(1)}) all-reduce(f32[16,101]{1,0:T(8,128)S(1)} %fusion.7, f32[16]{0:T(128)S(1)} %get-tuple-element.115, f32[16,101]{1,0:T(8,128)S(1)} %bitcast.173), channel_id=1, replica_groups=mesh['seq'=64,'head'=4] {'head'}, use_global_device_ids=true, to_apply=%region_15.16 | all-reduce | flops 3248 | bytes 25984 | tf_op jit(solution)/shard_map/psum | solution.py:202
  662.4 12.8 scatter_custom_fusion.1
  678.8 11.5 all-to-all-start.2
  693.8 40.9 %all-to-all-done.2 = bf16[64,50,256]{2,1,0:T(8,128)(2,1)S(1)} async-done(((bf16[64,50,256]{2,1,0:T(8,128)(2,1)}), bf16[64,50,256]{2,1,0:T(8,128)(2,1)S(1)}, u32[]{:S(2)}, u32[]{:S(2)}) %all-to-all-start.2) | async-done | bytes 1638432 | tf_op jit(solution)/shard_map/all_to_all | solution.py:220
  736.7 20.7 %scatter_custom_fusion.2 = f32[129,256]{1,0:T(8,128)S(1)} fusion(s32[3200]{0:T(1024)S(1)} %fusion.48, f32[3200,256]{1,0:T(8,128)} %reshape.314, f32[]{:T(128)} %constant.68.clone.1), kind=kCustom, calls=%fused_computation.78 | custom fusion | flops 819200 | bytes 132608 | tf_op jit(solution)/shard_map/scatter-add | solution.py:86
  758.1 540.6 %all-reduce.4.cloned.1.call-done = f32[960,256]{1,0:T(8,128)} async-done(((f32[960,256]{1,0:T(8,128)}), f32[960,256]{1,0:T(8,128)}) %all-reduce.4.cloned.1.call-update) | async-done | bytes 983056 | tf_op jit(solution)/shard_map/psum | solution.py:234
  (234 shorter events, 70.5 us)
Async XLA Ops:
  7.2 597.1 %copy-start = (bf16[240,960]{1,0:T(8,128)(2,1)S(1)}, bf16[240,960]{1,0:T(8,128)(2,1)}, u32[]{:S(2)}) copy-start(bf16[240,960]{1,0:T(8,128)(2,1)} %param.22) | copy-start | bytes 1382404
  7.2 315.4 %all-gather.7.cloned.1.call-start = ((), (), s32[]{:S(2)}) async-start(), calls=%async_computation.5 | async-start | bytes 3993600 | tf_op jit(solution)/shard_map/all_gather | solution.py:136
  8.2 19.0 %collective-permute-start = (bf16[64,240]{0,1:T(8,128)(2,1)S(1)}, bf16[64,240]{0,1:T(8,128)(2,1)S(1)}, u32[]{:S(2)}, u32[]{:S(2)}) collective-permute-start(bf16[64,240]{0,1:T(8,128)(2,1)S(1)} %get-tuple-element.106), channel_id=1, source_target_pairs={{0,4},{4,8},{8,12},{12,16},{16,20},{20,24},{24,28},{28,32},{32,36}... | collective-permute-start | bytes 92168 | tf_op jit(solution)/shard_map/ppermute | solution.py:20
  11.6 15.6 %collective-permute-start.1 = (bf16[64,240]{0,1:T(8,128)(2,1)S(1)}, bf16[64,240]{0,1:T(8,128)(2,1)S(1)}, u32[]{:S(2)}, u32[]{:S(2)}) collective-permute-start(bf16[64,240]{0,1:T(8,128)(2,1)S(1)} %get-tuple-element.107), channel_id=1, source_target_pairs={{4,0},{8,4},{12,8},{16,12},{20,16},{24,20},{28,24},{32,28},{36,32}... | collective-permute-start | bytes 92168 | tf_op jit(solution)/shard_map/ppermute | solution.py:21
  15.0 10.8 copy-start.5
  25.7 1.5 copy-start.3
  27.6 25.3 %copy-start.12 = (f32[960]{0:T(1024)S(1)}, f32[960]{0:T(1024)}, u32[]{:S(2)}) copy-start(f32[960]{0:T(1024)} %param.18) | copy-start | bytes 11524
  27.6 25.3 %copy-start.13 = (f32[960]{0:T(1024)S(1)}, f32[960]{0:T(1024)}, u32[]{:S(2)}) copy-start(f32[960]{0:T(1024)} %param.17) | copy-start | bytes 11524
  44.9 9.4 copy-start.6
  54.1 3.0 copy-start.10
  54.1 516.2 %all-gather.5.cloned.1.call-start = ((), (), s32[]{:S(2)}) async-start(), calls=%async_computation.4 | async-start | bytes 3993600 | tf_op jit(solution)/shard_map/all_gather | solution.py:135
  75.8 23.3 %copy-start.7 = (bf16[2,115200]{1,0:T(2,128)(2,1)S(1)}, bf16[2,115200]{1,0:T(2,128)(2,1)}, u32[]{:S(2)}) copy-start(bf16[2,115200]{1,0:T(2,128)(2,1)} %param.19) | copy-start | bytes 1382404
  76.4 33.5 %copy-start.1 = (bf16[128,256]{1,0:T(8,128)(2,1)S(1)}, bf16[128,256]{1,0:T(8,128)(2,1)}, u32[]{:S(2)}) copy-start(bf16[128,256]{1,0:T(8,128)(2,1)} %param.24) | copy-start | bytes 196612
  86.3 22.2 %all-to-all-start = ((s32[64,1,50]{2,1,0:T(1,128)}), s32[64,1,50]{2,1,0:T(1,128)S(1)}, u32[]{:S(2)}, u32[]{:S(2)}) async-start(s32[64,1,50]{2,1,0:T(1,128)} %bitcast.24), calls=%async_computation.1 | async-start | bytes 65536 | tf_op jit(solution)/shard_map/all_to_all | solution.py:192
  121.4 484.6 %all-to-all-start.1 = ((bf16[64,50,256]{2,1,0:T(8,128)(2,1)}), bf16[64,50,256]{2,1,0:T(8,128)(2,1)}, u32[]{:S(2)}, u32[]{:S(2)}) async-start(bf16[64,50,256]{2,1,0:T(8,128)(2,1)} %reshape.279), calls=%async_computation.2 | async-start | bytes 3670016 | tf_op jit(solution)/shard_map/all_to_all | solution.py:194
  127.7 507.9 %reduce-scatter.2.cloned.1.call-start = ((), (), s32[]{:S(2)}) async-start(), calls=%async_computation.6 | async-start | bytes 307200 | tf_op jit(solution)/shard_map/reduce_scatter | solution.py:160
  574.8 30.6 %copy-start.14 = (s32[16]{0:T(128)S(1)}, s32[16]{0:T(128)}, u32[]{:S(2)}) copy-start(s32[16]{0:T(128)} %param.25) | copy-start | bytes 196
  614.1 29.9 %copy-start.4 = (bf16[960,256]{1,0:T(8,128)(2,1)S(1)}, bf16[960,256]{1,0:T(8,128)(2,1)}, u32[]{:S(2)}) copy-start(bf16[960,256]{1,0:T(8,128)(2,1)} %param.23) | copy-start | bytes 1474564
  614.3 44.5 %copy-start.11 = (f32[16]{0:T(128)S(1)}, f32[16]{0:T(128)}, u32[]{:S(2)}) copy-start(f32[16]{0:T(128)} %param.27) | copy-start | bytes 196
  636.4 23.3 %copy-start.8 = (bf16[128,240]{0,1:T(8,128)(2,1)}, bf16[128,240]{0,1:T(8,128)(2,1)S(1)}, u32[]{:S(2)}) copy-start(bf16[128,240]{0,1:T(8,128)(2,1)S(1)} %add_convert_fusion) | copy-start | bytes 184324
  659.7 1.2 copy-start.2
  678.8 56.0 %all-to-all-start.2 = ((bf16[64,50,256]{2,1,0:T(8,128)(2,1)}), bf16[64,50,256]{2,1,0:T(8,128)(2,1)S(1)}, u32[]{:S(2)}, u32[]{:S(2)}) async-start(bf16[64,50,256]{2,1,0:T(8,128)(2,1)} %convert_element_type.74), calls=%async_computation.3 | async-start | bytes 3670016 | tf_op jit(solution)/shard_map/all_to_all | solution.py:220
  690.2 608.5 %all-reduce.4.cloned.1.call-start = ((), (), s32[]{:S(2)}) async-start(), calls=%async_computation.7 | async-start | bytes 1966080 | tf_op jit(solution)/shard_map/psum | solution.py:234
  758.1 542.8 %copy-start.9 = (f32[128,256]{1,0:T(8,128)}, f32[128,256]{1,0:T(8,128)S(1)}, u32[]{:S(2)}) copy-start(f32[128,256]{1,0:T(8,128)S(1)} %scatter_custom_fusion.3) | copy-start | bytes 393220
Sparse Core Ops, SparseCore 0:
  54.2 268.2 all-gather.6
  324.8 245.4 all-gather.4
  605.4 30.1 reduce-scatter.1
  694.2 604.5 all-reduce.3
where the time goes:
time: 1310 us
  waiting for transfers between devices  1050 us (80%)
  local copies, waits for them, and re-layouts  97.4 us (7%)
  other arithmetic  49.3 us (4%)
  starting transfers between devices  38.1 us (3%)
  matrix products  32.3 us (2%)
  blocking collectives  27.5 us (2%)
  between operations  14.4 us (1%)
    psum x1, waiting for transfers between devices, per_device(): proj_grad = lax.psum(proj_term, 'seq')  541 us
    all_gather x1, waiting for transfers between devices, per_device(): key_piece = lax.all_gather(key_here, 'seq', axis=0, tiled=True)  243 us
    all_gather x1, waiting for transfers between devices, per_device(): value_piece = lax.all_gather(value_here, 'seq', axis=0, tiled=True)  194 us
    all_to_all x1, waiting for transfers between devices, per_device(): lax.all_to_all(outgoing.reshape(seq_count, capacity, target_width).astype...  40.9 us
  transfers between devices with their start and end apart: 9, of which 6 were waited for; matrix products, arithmetic and copies ran while one was open for 10% of the time, Pallas kernels for 0%

commit v1 on v0

--- a/solution.py
+++ b/solution.py
@@ -132,7 +132,9 @@
         jnp.full((head_count, frame_count), -1e30, jnp.float32),
     )
     running = initial
-    key_piece = lax.all_gather(key_here, "seq", axis=0, tiled=True)
+    key_piece = jnp.concatenate(
+        lax.all_to_all(jnp.stack([key_here] * lax.axis_size("seq")), "seq", 0, 0), axis=0
+    )
     value_piece = lax.all_gather(value_here, "seq", axis=0, tiled=True)
     row_count = key_piece.shape[0]
 

time: 1310 us -> 1170 us (0.89)
  waiting for transfers between devices: 1050 us -> 868 us
  local copies, waits for them, and re-layouts: 97.4 us -> 116 us
  starting transfers between devices: 38.1 us -> 54.4 us
    all_gather x1 -> x0, waiting for transfers between devices: 243 us -> none  [per_device(): key_piece = lax.all_gather(key_here, 'seq', axis=0, tiled=True)]
    all_gather x1, waiting for transfers between devices: 194 us -> 257 us  [per_device(): value_piece = lax.all_gather(value_here, 'seq', axis=0, tiled=True)]
  transfers between devices with their start and end apart: 9 -> 9, of which waited for: 6 -> 4; matrix products, arithmetic and copies ran while one was open for 10% -> 15% of each run, Pallas kernels for 0% -> 0%
where the time goes in v1:
time: 1170 us; the launch traced here: 1160 us
  waiting for transfers between devices  868 us (74%)
  local copies, waits for them, and re-layouts  116 us (10%)
  starting transfers between devices  54.4 us (5%)
  other arithmetic  48.6 us (4%)
  matrix products  32.3 us (3%)
  blocking collectives  28 us (2%)
  between operations  14.6 us (1%)
    psum x1, waiting for transfers between devices, per_device(): proj_grad = lax.psum(proj_term, 'seq')  541 us
    all_gather x1, waiting for transfers between devices, per_device(): value_piece = lax.all_gather(value_here, 'seq', axis=0, tiled=True)  257 us
    all_to_all x1, waiting for transfers between devices, per_device(): lax.all_to_all(outgoing.reshape(seq_count, capacity, target_width).astype...  41.1 us
    reduce_scatter x1, waiting for transfers between devices, per_device(): lax.psum_scatter(jnp.dot(attended, out_weight, preferred_element_type=jnp...  29.2 us
  transfers between devices with their start and end apart: 9, of which 4 were waited for; matrix products, arithmetic and copies ran while one was open for 15% of the time, Pallas kernels for 0%

profile of v1, /device:TPU:8, one launch (start us, length us, event | category | flops | bytes accessed | tf_op | source)
XLA Modules:
  0.0 1162.8 jit_solution(13233743577178564869)
XLA Ops:
  16.7 18.1 %reduce-window.6 = s32[64,13,128]{2,1,0:T(8,128)S(1)} reduce-window(s32[64,13,128]{2,1,0:T(8,128)S(1)} %reshape.253, s32[]{:T(128)} %constant.57.clone.1), window={size=1x1x128 pad=0_0x0_0x127_0}, to_apply=%region_7.8 | reduce-window | flops 13524992 | bytes 851972 | tf_op jit(solution)/shard_map/reduce-window
  36.0 8.8 scatter_custom_fusion
  45.6 12.8 %all-to-all-start.1 = ((s32[64,1,50]{2,1,0:T(1,128)}), s32[64,1,50]{2,1,0:T(1,128)S(1)}, u32[]{:S(2)}, u32[]{:S(2)}) async-start(s32[64,1,50]{2,1,0:T(1,128)} %bitcast.24), calls=%async_computation.2 | async-start | bytes 65536 | tf_op jit(solution)/shard_map/all_to_all | solution.py:194
  58.7 10.7 copy.42
  72.9 17.3 %fusion.67 = f32[1,129,2,120]{3,0,2,1:T(1,128)S(1)} fusion(bf16[1,256,2,120]{3,0,2,1:T(2,128)(2,1)S(1)} %copy.41, bf16[2,120,120,128]{2,1,0,3:T(8,128)(2,1)} %copy.42), kind=kOutput, calls=%fused_computation.134 | convolution fusion | flops 951091200 | bytes 7619520 | tf_op jit(solution)/shard_map/conv_general_dilated | solution.py:108
  90.6 7.8 all_gather.9
  102.9 11.5 all-to-all-start
  117.5 9.9 gather_fusion.2
  129.4 257.1 %all-gather.4.cloned.1.call-done = bf16[8192,240]{0,1:T(8,128)(2,1)} async-done(((bf16[128,240]{0,1:T(8,128)(2,1)}), bf16[8192,240]{0,1:T(8,128)(2,1)}) %all-gather.4.cloned.1.call-update) | async-done | bytes 3932176 | tf_op jit(solution)/shard_map/all_gather | solution.py:138
  386.5 4.4 copy.77
  390.9 11.3 all-to-all-start.2
  402.5 5.1 copy.45
  407.6 7.2 reshape_reshape.3
  414.8 6.3 copy.48
  421.1 29.4 %while.15 = (s32[]{:T(128)}, f32[2,128,120]{1,2,0:T(8,128)S(1)}, f32[2,128]{1,0:T(2,128)S(1)}, f32[2,128]{1,0:T(2,128)S(1)}, bf16[16,512,240]{1,2,0:T(8,128)(2,1...) while((s32[]{:T(128)}, f32[2,128,120]{1,2,0:T(8,128)S(1)}, ...), condition=%wide.region_5.6_spmd.clone, body=%wide.region_2.5_spmd.clone.sunk | while | flops 63794432 | bytes 3371117 | solution.py:147
  454.8 5.6 gather_fusion.3
  461.0 29.2 %reduce-scatter.2.cloned.1.call-done = bf16[128,240]{0,1:T(8,128)(2,1)} async-done(((bf16[128,960]{0,1:T(8,128)(2,1)}), bf16[128,240]{0,1:T(8,128)(2,1)}) %reduce-scatter.2.cloned.1.call-update) | async-done | bytes 61456 | tf_op jit(solution)/shard_map/reduce_scatter | solution.py:162
  491.8 6.7 all-gather.1
  499.7 13.5 %all-reduce.1 = (f32[16,101]{1,0:T(8,128)S(1)}, f32[16]{0:T(128)S(1)}, f32[16,101]{1,0:T(8,128)S(1)}) all-reduce(f32[16,101]{1,0:T(8,128)S(1)} %fusion.7, f32[16]{0:T(128)S(1)} %get-tuple-element.115, f32[16,101]{1,0:T(8,128)S(1)} %bitcast.169), channel_id=1, replica_groups=mesh['seq'=64,'head'=4] {'head'}, use_global_device_ids=true, to_apply=%region_15.16 | all-reduce | flops 3248 | bytes 25984 | tf_op jit(solution)/shard_map/psum | solution.py:204
  517.1 13.0 %scatter_custom_fusion.1 = f32[3200,256]{1,0:T(8,128)} fusion(s32[1600]{0:T(1024)S(1)} %fusion.54, f32[1600,256]{1,0:T(8,128)} %reshape.300, f32[]{:T(128)} %constant.68.clone.1), kind=kCustom, calls=%fused_computation.28 | custom fusion | bytes 3277312 | tf_op jit(solution)/shard_map/scatter | solution.py:219
  533.6 11.5 all-to-all-start.3
  548.4 41.1 %all-to-all-done.3 = bf16[64,50,256]{2,1,0:T(8,128)(2,1)S(1)} async-done(((bf16[64,50,256]{2,1,0:T(8,128)(2,1)}), bf16[64,50,256]{2,1,0:T(8,128)(2,1)S(1)}, u32[]{:S(2)}, u32[]{:S(2)}) %all-to-all-start.3) | async-done | bytes 1638432 | tf_op jit(solution)/shard_map/all_to_all | solution.py:222
  591.4 20.7 %scatter_custom_fusion.2 = f32[129,256]{1,0:T(8,128)S(1)} fusion(s32[3200]{0:T(1024)S(1)} %fusion.48, f32[3200,256]{1,0:T(8,128)} %reshape.308, f32[]{:T(128)} %constant.68.clone.1), kind=kCustom, calls=%fused_computation.77 | custom fusion | flops 819200 | bytes 132608 | tf_op jit(solution)/shard_map/scatter-add | solution.py:86
  612.9 540.9 %all-reduce.4.cloned.1.call-done = f32[960,256]{1,0:T(8,128)} async-done(((f32[960,256]{1,0:T(8,128)}), f32[960,256]{1,0:T(8,128)}) %all-reduce.4.cloned.1.call-update) | async-done | bytes 983056 | tf_op jit(solution)/shard_map/psum | solution.py:236
  (234 shorter events, 76.9 us)
Async XLA Ops:
  7.2 443.4 %copy-start = (bf16[240,960]{1,0:T(8,128)(2,1)S(1)}, bf16[240,960]{1,0:T(8,128)(2,1)}, u32[]{:S(2)}) copy-start(bf16[240,960]{1,0:T(8,128)(2,1)} %param.22) | copy-start | bytes 1382404
  8.2 64.3 %collective-permute-start = (bf16[64,240]{0,1:T(8,128)(2,1)S(1)}, bf16[64,240]{0,1:T(8,128)(2,1)S(1)}, u32[]{:S(2)}, u32[]{:S(2)}) collective-permute-start(bf16[64,240]{0,1:T(8,128)(2,1)S(1)} %get-tuple-element.106), channel_id=1, source_target_pairs={{0,4},{4,8},{8,12},{12,16},{16,20},{20,24},{24,28},{28,32},{32,36}... | collective-permute-start | bytes 92168 | tf_op jit(solution)/shard_map/ppermute | solution.py:20
  11.6 60.9 %collective-permute-start.1 = (bf16[64,240]{0,1:T(8,128)(2,1)S(1)}, bf16[64,240]{0,1:T(8,128)(2,1)S(1)}, u32[]{:S(2)}, u32[]{:S(2)}) collective-permute-start(bf16[64,240]{0,1:T(8,128)(2,1)S(1)} %get-tuple-element.107), channel_id=1, source_target_pairs={{4,0},{8,4},{12,8},{16,12},{20,16},{24,20},{28,24},{32,28},{36,32}... | collective-permute-start | bytes 92168 | tf_op jit(solution)/shard_map/ppermute | solution.py:21
  45.6 54.8 %all-to-all-start.1 = ((s32[64,1,50]{2,1,0:T(1,128)}), s32[64,1,50]{2,1,0:T(1,128)S(1)}, u32[]{:S(2)}, u32[]{:S(2)}) async-start(s32[64,1,50]{2,1,0:T(1,128)} %bitcast.24), calls=%async_computation.2 | async-start | bytes 65536 | tf_op jit(solution)/shard_map/all_to_all | solution.py:194
  58.4 328.2 %all-gather.4.cloned.1.call-start = ((), (), s32[]{:S(2)}) async-start(), calls=%async_computation.5 | async-start | bytes 3993600 | tf_op jit(solution)/shard_map/all_gather | solution.py:138
  58.7 10.8 copy-start.5
  69.5 1.5 copy-start.6
  69.5 3.1 copy-start.3
  72.8 25.8 %copy-start.11 = (f32[960]{0:T(1024)S(1)}, f32[960]{0:T(1024)}, u32[]{:S(2)}) copy-start(f32[960]{0:T(1024)} %param.18) | copy-start | bytes 11524
  72.8 25.8 %copy-start.12 = (f32[960]{0:T(1024)S(1)}, f32[960]{0:T(1024)}, u32[]{:S(2)}) copy-start(f32[960]{0:T(1024)} %param.17) | copy-start | bytes 11524
  102.9 11.6 copy-start.7
  102.9 288.1 %all-to-all-start = ((bf16[64,128,240]{1,2,0:T(8,128)(2,1)}), bf16[64,128,240]{1,2,0:T(8,128)(2,1)}, u32[]{:S(2)}, u32[]{:S(2)}) async-start(bf16[64,128,240]{1,2,0:T(8,128)(2,1)} %stack.3), calls=%async_computation | async-start | bytes 7864320 | tf_op jit(solution)/shard_map/all_to_all | solution.py:136
  114.4 3.1 copy-start.1
  390.9 61.4 %all-to-all-start.2 = ((bf16[64,50,256]{2,1,0:T(8,128)(2,1)}), bf16[64,50,256]{2,1,0:T(8,128)(2,1)}, u32[]{:S(2)}, u32[]{:S(2)}) async-start(bf16[64,50,256]{2,1,0:T(8,128)(2,1)} %reshape.273), calls=%async_computation.3 | async-start | bytes 3670016 | tf_op jit(solution)/shard_map/all_to_all | solution.py:196
  402.3 88.0 %reduce-scatter.2.cloned.1.call-start = ((), (), s32[]{:S(2)}) async-start(), calls=%async_computation.6 | async-start | bytes 307200 | tf_op jit(solution)/shard_map/reduce_scatter | solution.py:162
  421.1 30.6 %copy-start.13 = (s32[16]{0:T(128)S(1)}, s32[16]{0:T(128)}, u32[]{:S(2)}) copy-start(s32[16]{0:T(128)} %param.25) | copy-start | bytes 196
  460.4 38.2 %copy-start.4 = (bf16[960,256]{1,0:T(8,128)(2,1)S(1)}, bf16[960,256]{1,0:T(8,128)(2,1)}, u32[]{:S(2)}) copy-start(bf16[960,256]{1,0:T(8,128)(2,1)} %param.23) | copy-start | bytes 1474564
  460.6 52.8 %copy-start.10 = (f32[16]{0:T(128)S(1)}, f32[16]{0:T(128)}, u32[]{:S(2)}) copy-start(f32[16]{0:T(128)} %param.27) | copy-start | bytes 196
  491.1 23.3 %copy-start.8 = (bf16[128,240]{0,1:T(8,128)(2,1)}, bf16[128,240]{0,1:T(8,128)(2,1)S(1)}, u32[]{:S(2)}) copy-start(bf16[128,240]{0,1:T(8,128)(2,1)S(1)} %add_convert_fusion) | copy-start | bytes 184324
  514.4 1.2 copy-start.2
  533.6 55.9 %all-to-all-start.3 = ((bf16[64,50,256]{2,1,0:T(8,128)(2,1)}), bf16[64,50,256]{2,1,0:T(8,128)(2,1)S(1)}, u32[]{:S(2)}, u32[]{:S(2)}) async-start(bf16[64,50,256]{2,1,0:T(8,128)(2,1)} %convert_element_type.74), calls=%async_computation.4 | async-start | bytes 3670016 | tf_op jit(solution)/shard_map/all_to_all | solution.py:222
  545.1 608.8 %all-reduce.4.cloned.1.call-start = ((), (), s32[]{:S(2)}) async-start(), calls=%async_computation.7 | async-start | bytes 1966080 | tf_op jit(solution)/shard_map/psum | solution.py:236
  612.9 543.1 %copy-start.9 = (f32[128,256]{1,0:T(8,128)}, f32[128,256]{1,0:T(8,128)S(1)}, u32[]{:S(2)}) copy-start(f32[128,256]{1,0:T(8,128)S(1)} %scatter_custom_fusion.3) | copy-start | bytes 393220
Sparse Core Ops, SparseCore 0:
  100.0 286.5 all-gather.3
  451.8 38.4 reduce-scatter.1
  549.3 604.4 all-reduce.3
